TPU v7x, 512 devices: a whole 4x8x8 slice. The times are simulated.
512 devices in a mesh: space: 64 (over z_lo, y, core), chan: 8 (over x, z_hi).
Axes of the slice: x: 4, y: 8, z: 8 (z_hi: 2, z_lo: 4; z = z_hi * 4 + z_lo), core: 2. Of those that a mesh axis runs over, the one named last changes fastest.
Arguments:
- features: bfloat16 [1, 128, 128, 2048], P(None, 'chan', 'space'), may hold values from -6 to 6
- top_map: int32 [64, 2048], P('space'), may hold values from 0 to 2048, as said below
- bottom_map: int32 [64, 2048], P('space'), may hold values from 0 to 2048, as said below
- first_weight: bfloat16 [128, 3, 3, 128], P('chan'), may hold values from -0.1875 to 0.1875
- first_bias: float32 [128], P('chan'), may hold values from -3 to 3
- second_weight: bfloat16 [256, 3, 3, 128], P('chan'), may hold values from -0.1875 to 0.1875
- second_bias: float32 [256], P('chan'), may hold values from -3 to 3
Outputs:
- hidden: bfloat16 [1, 128, 128, 2048], P(None, 'chan', 'space')
- coarse: bfloat16 [1, 256, 64, 1024], P(None, 'chan', 'space')
Inputs may be any that keep to these rules, and one draw needn't show every extreme that they name: `top_map`: each entry of row s, column k is k - 1, k or k + 1 taken modulo 2048, or 2048 for a missing neighbour at a face corner; exactly 4 entries of each row equal 2048. `bottom_map`: each entry of row s, column k is k - 1, k or k + 1 taken modulo 2048, or 2048 for a missing neighbour at a face corner; exactly 4 entries of each row equal 2048.
All inputs are finite; a program needn't handle non-finite values.
Results may differ from a plain program's by a relative error of at most 0.012.
Values may be sent and summed in bfloat16 or wider, within the bound.
No kernel may reach another device: no remote copies, remote signals or barrier semaphores. Data moves between devices by JAX's collectives and lax.ppermute only.
A program may use at most 64 MiB of HBM per device.

v0:
```python
import jax
import jax.numpy as jnp
from jax import lax
from jax.sharding import PartitionSpec as P


def with_halo(cells, sides, width):
    for axis, dim in sides:
        count = lax.axis_size(axis)
        ends = count - 1
        head = lax.slice_in_dim(cells, 0, width, axis=dim)
        tail = lax.slice_in_dim(cells, cells.shape[dim] - width, cells.shape[dim], axis=dim)
        cells = jnp.concatenate(
            [
                lax.ppermute(tail, axis, [(i, (i + 1) % count) for i in range(ends)]),
                cells,
                lax.ppermute(head, axis, [((i + 1) % count, i) for i in range(ends)]),
            ],
            axis=dim,
        )
    return cells


def shifted_2(array, axis, by):
    devices = lax.axis_size(axis)
    pairs = [(i, i + by) for i in range(devices) if 0 <= i + by < devices]
    return lax.ppermute(array, axis, pairs)


def remap_row(source_row, table):
    zero_col = jnp.zeros(source_row.shape[:-1] + (1,), source_row.dtype)
    return jnp.take(jnp.concatenate([source_row, zero_col], axis=-1), table, axis=-1)


def per_device(features, top_map, bottom_map, first_weight, first_bias, second_weight, second_bias):
    row_count = features.shape[2]
    cycle_width = features.shape[3]
    upper_map = top_map[0]
    lower_map = bottom_map[0]
    gathered = lax.all_gather(features, "chan", axis=1, tiled=True)
    framed = with_halo(gathered, (("space", 2),), 1)
    above_row = remap_row(framed[:, :, 0, :], upper_map)
    below_row = remap_row(framed[:, :, row_count + 1, :], lower_map)
    padded = jnp.concatenate([above_row[:, :, None], gathered, below_row[:, :, None]], 2)
    totals = jnp.zeros(
        (features.shape[0], first_weight.shape[0], row_count, cycle_width), jnp.float32
    )
    for row_step in range(3):
        for col_step in range(3):
            shifted = jnp.roll(
                padded[:, :, row_step : row_step + row_count, :], 1 - col_step, axis=3
            )
            totals = totals + jnp.einsum(
                "oc,bcrw->borw",
                first_weight[:, row_step, col_step, :],
                shifted,
                preferred_element_type=jnp.float32,
            )
    hidden = jax.nn.gelu(totals + first_bias[None, :, None, None]).astype(jnp.bfloat16)
    half_rows = row_count // 2
    gathered_hidden = lax.all_gather(hidden, "chan", axis=1, tiled=True)
    rim_row = shifted_2(gathered_hidden[:, :, row_count - 1, :], "space", 1)
    stacked = jnp.concatenate([remap_row(rim_row, upper_map)[:, :, None], gathered_hidden], 2)
    sums = jnp.zeros(
        (hidden.shape[0], second_weight.shape[0], half_rows, cycle_width // 2), jnp.float32
    )
    for row_step in range(3):
        for col_step in range(3):
            picked = jnp.roll(
                stacked[:, :, row_step : row_step + row_count : 2, :], 1 - col_step, axis=3
            )[..., ::2]
            sums = sums + jnp.einsum(
                "oc,bcrw->borw",
                second_weight[:, row_step, col_step, :],
                picked,
                preferred_element_type=jnp.float32,
            )
    coarse = jax.nn.gelu(sums + second_bias[None, :, None, None]).astype(jnp.bfloat16)
    return (hidden, coarse)


def solution(mesh):
    placed = (
        P(None, "chan", "space", None),
        P("space", None),
        P("space", None),
        P("chan", None, None, None),
        P("chan"),
        P("chan", None, None, None),
        P("chan"),
    )
    return jax.shard_map(
        per_device,
        mesh=mesh,
        in_specs=placed,
        out_specs=(P(None, "chan", "space", None), P(None, "chan", "space", None)),
        check_vma=False,
    )
```

profile of v0, /device:TPU:25, one launch (start us, length us, event | category | flops | bytes accessed | tf_op | source)
XLA Modules:
  0.0 264.1 jit_solution(7621877287431449558)
XLA Ops:
  7.2 1.6 copy.9
  8.9 0.7 compare_and_fusion.1
  9.6 0.7 fusion.97
  10.3 72.2 %all-gather.3.cloned.1.call-done = bf16[1,128,2,2048]{3,1,2,0:T(8,128)(2,1)} async-done(((bf16[1,16,2,2048]{3,1,2,0:T(8,128)(2,1)}), bf16[1,128,2,2048]{3,1,2,0:T(8,128)(2,1)}) %all-gather.3.cloned.1.call-update) | async-done | bytes 1048592 | tf_op jit(solution)/shard_map/all_gather | solution.py:40
  82.5 2.2 fusion.128
  84.7 6.3 %collective-permute-start = (bf16[1,128,1,2048]{3,1,2,0:T(8,128)(2,1)S(1)}, bf16[1,128,1,2048]{3,1,2,0:T(8,128)(2,1)S(1)}, u32[]{:S(2)}, u32[]{:S(2)}) collective-permute-start(bf16[1,128,1,2048]{3,1,2,0:T(8,128)(2,1)S(1)} %get-tuple-element.25), channel_id=1, source_target_pairs={{0,8},{8,16},{16,24},{24,32},{32,40},{40,48},{48,56},{56,64},{64,7... | collective-permute-start | bytes 1572872 | tf_op jit(solution)/shard_map/ppermute | solution.py:15
  91.0 1.9 collective-permute-start.1
  93.0 4.0 %collective-permute-done = bf16[1,128,1,2048]{3,1,2,0:T(8,128)(2,1)S(1)} collective-permute-done((bf16[1,128,1,2048]{3,1,2,0:T(8,128)(2,1)S(1)}, bf16[1,128,1,2048]{3,1,2,0:T(8,128)(2,1)S(1)}, u32[]{:S(2)}, u32[]{:S(2)}) %collective-permute-start) | collective-permute-done | bytes 524320 | tf_op jit(solution)/shard_map/ppermute | solution.py:15
  97.4 6.2 %gather_fusion = bf16[2048,128]{1,0:T(8,128)(2,1)S(1)} fusion(bf16[128,2049]{0,1:T(8,128)(2,1)S(1)} %copy.10, s32[2048]{0:T(1024)S(1)} %fusion.97), kind=kCustom, calls=%fused_computation.clone | custom fusion | bytes 1056768 | tf_op jit(solution)/shard_map/jit(_take)/gather | solution.py:32
  104.2 6.2 %gather_fusion.1 = bf16[2048,128]{1,0:T(8,128)(2,1)S(1)} fusion(bf16[128,2049]{0,1:T(8,128)(2,1)S(1)} %copy.12, s32[2048]{0:T(1024)S(1)} %fusion.98), kind=kCustom, calls=%fused_computation.1.clone | custom fusion | bytes 1056768 | tf_op jit(solution)/shard_map/jit(_take)/gather | solution.py:32
  110.7 1.4 fusion.6
  112.2 0.5 fusion.30
  113.2 0.5 convolution_add_fusion.5
  114.2 0.5 convolution_add_fusion.2
  115.4 0.9 fusion.54
  116.3 1.7 copy.15
  118.0 61.1 %all-gather.5.cloned.1.call-done = bf16[1,128,2,2048]{3,1,2,0:T(8,128)(2,1)} async-done(((bf16[1,16,2,2048]{3,1,2,0:T(8,128)(2,1)}), bf16[1,128,2,2048]{3,1,2,0:T(8,128)(2,1)}) %all-gather.5.cloned.1.call-update) | async-done | bytes 1048592 | tf_op jit(solution)/shard_map/all_gather | solution.py:61
  179.2 2.3 fusion.127
  181.4 6.3 %collective-permute-start.2 = (bf16[1,128,2048]{2,1,0:T(8,128)(2,1)}, bf16[1,128,2048]{2,1,0:T(8,128)(2,1)}, u32[]{:S(2)}, u32[]{:S(2)}) collective-permute-start(bf16[1,128,2048]{2,1,0:T(8,128)(2,1)} %get-tuple-element.18), channel_id=1, source_target_pairs={{0,8},{8,16},{16,24},{24,32},{32,40},{40,48},{48,56},{56,64},{64,7... | collective-permute-start | bytes 1572872 | tf_op jit(solution)/shard_map/ppermute | solution.py:27
  187.7 0.5 fusion.125
  188.6 9.8 %slice.269 = bf16[1,128,1,1024]{3,1,2,0:T(8,128)(2,1)} slice(bf16[1,128,1,2048]{3,1,2,0:T(8,128)(2,1)S(1)} %pad_maximum_fusion.9), slice={[0:1:1], [0:128:1], [0:1:1], [0:2048:2]} | slice | bytes 524288 | tf_op jit(solution)/shard_map/slice | solution.py:69
  198.4 9.0 %slice.263 = bf16[1,128,1,1024]{3,1,2,0:T(8,128)(2,1)S(1)} slice(bf16[1,128,1,2048]{3,1,2,0:T(8,128)(2,1)S(1)} %pad_maximum_fusion.8), slice={[0:1:1], [0:128:1], [0:1:1], [0:2048:2]} | slice | bytes 524288 | tf_op jit(solution)/shard_map/slice | solution.py:69
  207.5 9.0 %slice.259 = bf16[1,128,1,1024]{3,1,2,0:T(8,128)(2,1)S(1)} slice(bf16[1,128,1,2048]{3,1,2,0:T(8,128)(2,1)S(1)} %pad_maximum_fusion.7), slice={[0:1:1], [0:128:1], [0:1:1], [0:2048:2]} | slice | bytes 524288 | tf_op jit(solution)/shard_map/slice | solution.py:69
  216.7 9.0 %slice.252 = bf16[1,128,1,1024]{3,1,2,0:T(8,128)(2,1)S(1)} slice(bf16[1,128,1,2048]{3,1,2,0:T(8,128)(2,1)S(1)} %pad_maximum_fusion.6), slice={[0:1:1], [0:128:1], [0:1:1], [0:2048:2]} | slice | bytes 524288 | tf_op jit(solution)/shard_map/slice | solution.py:69
  225.7 9.0 %slice.255 = bf16[1,128,1,1024]{3,1,2,0:T(8,128)(2,1)S(1)} slice(bf16[1,128,1,2048]{3,1,2,0:T(8,128)(2,1)S(1)} %get-tuple-element.19), slice={[0:1:1], [0:128:1], [0:1:1], [0:2048:2]} | slice | bytes 524288 | tf_op jit(solution)/shard_map/slice | solution.py:69
  234.7 9.2 %slice.265 = bf16[1,128,1,1024]{3,1,2,0:T(8,128)(2,1)S(1)} slice(bf16[1,128,1,2048]{3,1,2,0:T(8,128)(2,1)S(1)} %get-tuple-element.17), slice={[0:1:1], [0:128:1], [0:1:1], [0:2048:2]} | slice | bytes 524288 | tf_op jit(solution)/shard_map/slice | solution.py:69
  243.9 1.1 pad_bitcast_fusion
  245.3 6.2 %gather_fusion.2 = bf16[2048,128]{1,0:T(8,128)(2,1)S(1)} fusion(bf16[128,2049]{0,1:T(8,128)(2,1)S(1)} %copy.14, s32[2048]{0:T(1024)S(1)} %fusion.97), kind=kCustom, calls=%fused_computation.2.clone | custom fusion | bytes 1056768 | tf_op jit(solution)/shard_map/jit(_take)/gather | solution.py:32
  252.0 0.8 slice.244
  252.9 0.8 slice.248
  253.8 0.8 slice.242
  256.4 0.8 fusion.76
  (56 shorter events, 6.6 us)
Async XLA Ops:
  7.2 75.3 %all-gather.3.cloned.1.call-start = ((), (), s32[]{:S(2)}) async-start(), calls=%async_computation | async-start | bytes 1179648 | tf_op jit(solution)/shard_map/all_gather | solution.py:40
  8.8 170.3 %all-gather.5.cloned.1.call-start = ((), (), s32[]{:S(2)}) async-start(), calls=%async_computation.1 | async-start | bytes 1179648 | tf_op jit(solution)/shard_map/all_gather | solution.py:61
  10.3 80.7 %copy-start.4 = (s32[1,2048]{1,0:T(1,128)S(1)}, s32[1,2048]{1,0:T(1,128)}, u32[]{:S(2)}) copy-start(s32[1,2048]{1,0:T(1,128)} %param.11) | copy-start | bytes 24580
  82.5 10.4 %copy-start = (bf16[1,128,2,2048]{3,1,2,0:T(8,128)(2,1)S(1)}, bf16[1,128,2,2048]{3,1,2,0:T(8,128)(2,1)}, u32[]{:S(2)}) copy-start(bf16[1,128,2,2048]{3,1,2,0:T(8,128)(2,1)} %all-gather.3.cloned.1.call-done) | copy-start | bytes 3145732
  84.7 12.4 %collective-permute-start = (bf16[1,128,1,2048]{3,1,2,0:T(8,128)(2,1)S(1)}, bf16[1,128,1,2048]{3,1,2,0:T(8,128)(2,1)S(1)}, u32[]{:S(2)}, u32[]{:S(2)}) collective-permute-start(bf16[1,128,1,2048]{3,1,2,0:T(8,128)(2,1)S(1)} %get-tuple-element.25), channel_id=1, source_target_pairs={{0,8},{8,16},{16,24},{24,32},{32,40},{40,48},{48,56},{56,64},{64,7... | collective-permute-start | bytes 1572872 | tf_op jit(solution)/shard_map/ppermute | solution.py:15
  91.0 12.8 %collective-permute-start.1 = (bf16[1,128,1,2048]{3,1,2,0:T(8,128)(2,1)}, bf16[1,128,1,2048]{3,1,2,0:T(8,128)(2,1)S(1)}, u32[]{:S(2)}, u32[]{:S(2)}) collective-permute-start(bf16[1,128,1,2048]{3,1,2,0:T(8,128)(2,1)} %get-tuple-element.24), channel_id=1, source_target_pairs={{8,0},{16,8},{24,16},{32,24},{40,32},{48,40},{56,48},{64,56},{72,6... | collective-permute-start | bytes 1572872 | tf_op jit(solution)/shard_map/ppermute | solution.py:17
  110.7 1.4 copy-start.5
  114.7 0.7 copy-start.6
  179.1 8.6 %copy-start.1 = (bf16[1,128,2,2048]{3,1,2,0:T(8,128)(2,1)S(1)}, bf16[1,128,2,2048]{3,1,2,0:T(8,128)(2,1)}, u32[]{:S(2)}) copy-start(bf16[1,128,2,2048]{3,1,2,0:T(8,128)(2,1)} %all-gather.5.cloned.1.call-done) | copy-start | bytes 3145732
  181.4 62.4 %collective-permute-start.2 = (bf16[1,128,2048]{2,1,0:T(8,128)(2,1)}, bf16[1,128,2048]{2,1,0:T(8,128)(2,1)}, u32[]{:S(2)}, u32[]{:S(2)}) collective-permute-start(bf16[1,128,2048]{2,1,0:T(8,128)(2,1)} %get-tuple-element.18), channel_id=1, source_target_pairs={{0,8},{8,16},{16,24},{24,32},{32,40},{40,48},{48,56},{56,64},{64,7... | collective-permute-start | bytes 1572872 | tf_op jit(solution)/shard_map/ppermute | solution.py:27
  252.9 1.8 copy-start.3
  255.4 1.0 copy-start.2
  255.4 0.9 copy-start.7
Sparse Core Ops, SparseCore 0:
  11.8 70.6 all-gather.2
  116.5 62.6 all-gather.4
where the time goes:
time: 264 us
  waiting for transfers between devices  137 us (52%)
  local copies, waits for them, and re-layouts  87.6 us (33%)
  starting transfers between devices  14.6 us (6%)
  between operations  14.4 us (5%)
  matrix products  5.98 us (2%)
  other arithmetic  4.09 us (2%)
    all_gather x1, waiting for transfers between devices, per_device(): gathered = lax.all_gather(features, 'chan', axis=1, tiled=True)  72.2 us
    all_gather x1, waiting for transfers between devices, per_device(): gathered_hidden = lax.all_gather(hidden, 'chan', axis=1, tiled=True)  61.1 us
    slice x13, local copies, waits for them, and re-layouts, per_device(): jnp.roll(stacked[:, :, row_step:row_step + row_count:2, :], 1 - col_step,...  58.1 us
    gather x5, local copies, waits for them, and re-layouts, remap_row(): jnp.take(jnp.concatenate([source_row, zero_col], axis=-1), table, axis=-1)  19 us
    ppermute x1, starting transfers between devices, shifted_2(): return lax.ppermute(array, axis, pairs)  6.29 us
    ppermute x1, starting transfers between devices, with_halo(): lax.ppermute(tail, axis, [(i, (i + 1) % count) for i in range(ends)])  6.29 us
  transfers between devices with their start and end apart: 5, of which 3 were waited for; matrix products, arithmetic and copies ran while one was open for 25% of the time, Pallas kernels for 0%

commit v1 on v0

--- a/solution.py
+++ b/solution.py
@@ -2,6 +2,13 @@
 import jax.numpy as jnp
 from jax import lax
 from jax.sharding import PartitionSpec as P
+
+
+def all_by_exchange(shard, name, dim):
+    devices = lax.axis_size(name)
+    pieces = jnp.stack([shard for _ in range(devices)])
+    pieces = lax.all_to_all(pieces, name, split_axis=0, concat_axis=0)
+    return jnp.concatenate(pieces, axis=dim)
 
 
 def with_halo(cells, sides, width):
@@ -37,7 +44,7 @@
     cycle_width = features.shape[3]
     upper_map = top_map[0]
     lower_map = bottom_map[0]
-    gathered = lax.all_gather(features, "chan", axis=1, tiled=True)
+    gathered = all_by_exchange(features, "chan", 1)
     framed = with_halo(gathered, (("space", 2),), 1)
     above_row = remap_row(framed[:, :, 0, :], upper_map)
     below_row = remap_row(framed[:, :, row_count + 1, :], lower_map)

time: 264 us -> 233 us (0.88)
  waiting for transfers between devices: 137 us -> 95.4 us
  starting transfers between devices: 14.6 us -> 26.9 us
    all_gather x1 -> x0, waiting for transfers between devices: 72.2 us -> none  [per_device(): gathered = lax.all_gather(features, 'chan', axis=1, tiled=True)]
    all_to_all x0 -> x1, waiting for transfers between devices: none -> 18.9 us  [all_by_exchange(): pieces = lax.all_to_all(pieces, name, split_axis=0, concat_axis=0)]
    all_to_all x0 -> x1, starting transfers between devices: none -> 12.6 us  [all_by_exchange(): pieces = lax.all_to_all(pieces, name, split_axis=0, concat_axis=0)]
    all_gather x1, waiting for transfers between devices: 61.1 us -> 72.5 us  [per_device(): gathered_hidden = lax.all_gather(hidden, 'chan', axis=1, tiled=True)]
  transfers between devices with their start and end apart: 5 -> 5, of which waited for: 3 -> 3; matrix products, arithmetic and copies ran while one was open for 25% -> 28% of each run, Pallas kernels for 0% -> 0%
where the time goes in v1:
time: 233 us; the launch traced here: 232 us
  waiting for transfers between devices  95.4 us (41%)
  local copies, waits for them, and re-layouts  86.9 us (37%)
  starting transfers between devices  26.9 us (12%)
  between operations  14.4 us (6%)
  matrix products  6 us (3%)
  other arithmetic  2.7 us (1%)
    all_gather x1, waiting for transfers between devices, per_device(): gathered_hidden = lax.all_gather(hidden, 'chan', axis=1, tiled=True)  72.5 us
    slice x13, local copies, waits for them, and re-layouts, per_device(): jnp.roll(stacked[:, :, row_step:row_step + row_count:2, :], 1 - col_step,...  58.1 us
    gather x5, local copies, waits for them, and re-layouts, remap_row(): jnp.take(jnp.concatenate([source_row, zero_col], axis=-1), table, axis=-1)  19 us
    all_to_all x1, waiting for transfers between devices, all_by_exchange(): pieces = lax.all_to_all(pieces, name, split_axis=0, concat_axis=0)  18.9 us
    all_to_all x1, starting transfers between devices, all_by_exchange(): pieces = lax.all_to_all(pieces, name, split_axis=0, concat_axis=0)  12.6 us
    ppermute x1, starting transfers between devices, shifted_2(): return lax.ppermute(array, axis, pairs)  6.29 us
    ppermute x1, starting transfers between devices, with_halo(): lax.ppermute(tail, axis, [(i, (i + 1) % count) for i in range(ends)])  6.1 us
  transfers between devices with their start and end apart: 5, of which 3 were waited for; matrix products, arithmetic and copies ran while one was open for 28% of the time, Pallas kernels for 0%

profile of v1, /device:TPU:25, one launch (start us, length us, event | category | flops | bytes accessed | tf_op | source)
XLA Modules:
  0.0 232.4 jit_solution(6403654930126534579)
XLA Ops:
  7.2 0.9 copy.16
  8.1 1.1 stack.2
  9.2 12.6 %all-to-all-start = ((bf16[8,1,16,2,2048]{4,2,3,1,0:T(8,128)(2,1)}), bf16[8,1,16,2,2048]{4,2,3,1,0:T(8,128)(2,1)S(1)}, u32[]{:S(2)}, u32[]{:S(2)}) async-start(bf16[8,1,16,2,2048]{4,2,3,1,0:T(8,128)(2,1)} %stack.2), calls=%async_computation | async-start | bytes 2097152 | tf_op jit(solution)/shard_map/all_to_all | solution.py:10
  21.9 18.9 %all-to-all-done = bf16[8,1,16,2,2048]{4,2,3,1,0:T(8,128)(2,1)S(1)} async-done(((bf16[8,1,16,2,2048]{4,2,3,1,0:T(8,128)(2,1)}), bf16[8,1,16,2,2048]{4,2,3,1,0:T(8,128)(2,1)S(1)}, u32[]{:S(2)}, u32[]{:S(2)}) %all-to-all-start) | async-done | bytes 1048608 | tf_op jit(solution)/shard_map/all_to_all | solution.py:10
  40.9 0.9 fusion.127
  41.8 6.1 %collective-permute-start = (bf16[1,128,1,2048]{3,1,2,0:T(8,128)(2,1)S(1)}, bf16[1,128,1,2048]{3,1,2,0:T(8,128)(2,1)S(1)}, u32[]{:S(2)}, u32[]{:S(2)}) collective-permute-start(bf16[1,128,1,2048]{3,1,2,0:T(8,128)(2,1)S(1)} %get-tuple-element.27), channel_id=1, source_target_pairs={{0,8},{8,16},{16,24},{24,32},{32,40},{40,48},{48,56},{56,64},{64,7... | collective-permute-start | bytes 1572872 | tf_op jit(solution)/shard_map/ppermute | solution.py:22
  47.9 1.9 collective-permute-start.1
  49.9 4.0 %collective-permute-done = bf16[1,128,1,2048]{3,1,2,0:T(8,128)(2,1)S(1)} collective-permute-done((bf16[1,128,1,2048]{3,1,2,0:T(8,128)(2,1)S(1)}, bf16[1,128,1,2048]{3,1,2,0:T(8,128)(2,1)S(1)}, u32[]{:S(2)}, u32[]{:S(2)}) %collective-permute-start) | collective-permute-done | bytes 524320 | tf_op jit(solution)/shard_map/ppermute | solution.py:22
  54.3 6.2 %gather_fusion = bf16[2048,128]{1,0:T(8,128)(2,1)S(1)} fusion(bf16[128,2049]{0,1:T(8,128)(2,1)S(1)} %copy.18, s32[2048]{0:T(1024)S(1)} %fusion.96), kind=kCustom, calls=%fused_computation.clone | custom fusion | bytes 1056768 | tf_op jit(solution)/shard_map/jit(_take)/gather | solution.py:39
  61.1 6.2 %gather_fusion.1 = bf16[2048,128]{1,0:T(8,128)(2,1)S(1)} fusion(bf16[128,2049]{0,1:T(8,128)(2,1)S(1)} %copy.21, s32[2048]{0:T(1024)S(1)} %fusion.97), kind=kCustom, calls=%fused_computation.1.clone | custom fusion | bytes 1056768 | tf_op jit(solution)/shard_map/jit(_take)/gather | solution.py:39
  67.6 1.4 fusion.6
  69.1 0.5 fusion.30
  70.1 0.5 convolution_add_fusion.5
  71.1 0.5 convolution_add_fusion.2
  72.3 1.0 fusion.53
  73.3 1.7 copy.24
  75.0 72.5 %all-gather.2.cloned.1.call-done = bf16[1,128,2,2048]{3,1,2,0:T(8,128)(2,1)} async-done(((bf16[1,16,2,2048]{3,1,2,0:T(8,128)(2,1)}), bf16[1,128,2,2048]{3,1,2,0:T(8,128)(2,1)}) %all-gather.2.cloned.1.call-update) | async-done | bytes 1048592 | tf_op jit(solution)/shard_map/all_gather | solution.py:68
  147.5 2.3 fusion.126
  149.7 6.3 %collective-permute-start.2 = (bf16[1,128,2048]{2,1,0:T(8,128)(2,1)}, bf16[1,128,2048]{2,1,0:T(8,128)(2,1)}, u32[]{:S(2)}, u32[]{:S(2)}) collective-permute-start(bf16[1,128,2048]{2,1,0:T(8,128)(2,1)} %get-tuple-element.20), channel_id=1, source_target_pairs={{0,8},{8,16},{16,24},{24,32},{32,40},{40,48},{48,56},{56,64},{64,7... | collective-permute-start | bytes 1572872 | tf_op jit(solution)/shard_map/ppermute | solution.py:34
  156.0 0.5 fusion.124
  156.9 9.8 %slice.269 = bf16[1,128,1,1024]{3,1,2,0:T(8,128)(2,1)} slice(bf16[1,128,1,2048]{3,1,2,0:T(8,128)(2,1)S(1)} %pad_maximum_fusion.9), slice={[0:1:1], [0:128:1], [0:1:1], [0:2048:2]} | slice | bytes 524288 | tf_op jit(solution)/shard_map/slice | solution.py:76
  166.7 9.0 %slice.263 = bf16[1,128,1,1024]{3,1,2,0:T(8,128)(2,1)S(1)} slice(bf16[1,128,1,2048]{3,1,2,0:T(8,128)(2,1)S(1)} %pad_maximum_fusion.8), slice={[0:1:1], [0:128:1], [0:1:1], [0:2048:2]} | slice | bytes 524288 | tf_op jit(solution)/shard_map/slice | solution.py:76
  175.8 9.0 %slice.259 = bf16[1,128,1,1024]{3,1,2,0:T(8,128)(2,1)S(1)} slice(bf16[1,128,1,2048]{3,1,2,0:T(8,128)(2,1)S(1)} %pad_maximum_fusion.7), slice={[0:1:1], [0:128:1], [0:1:1], [0:2048:2]} | slice | bytes 524288 | tf_op jit(solution)/shard_map/slice | solution.py:76
  185.0 9.0 %slice.252 = bf16[1,128,1,1024]{3,1,2,0:T(8,128)(2,1)S(1)} slice(bf16[1,128,1,2048]{3,1,2,0:T(8,128)(2,1)S(1)} %pad_maximum_fusion.6), slice={[0:1:1], [0:128:1], [0:1:1], [0:2048:2]} | slice | bytes 524288 | tf_op jit(solution)/shard_map/slice | solution.py:76
  194.0 9.0 %slice.255 = bf16[1,128,1,1024]{3,1,2,0:T(8,128)(2,1)S(1)} slice(bf16[1,128,1,2048]{3,1,2,0:T(8,128)(2,1)S(1)} %get-tuple-element.21), slice={[0:1:1], [0:128:1], [0:1:1], [0:2048:2]} | slice | bytes 524288 | tf_op jit(solution)/shard_map/slice | solution.py:76
  203.0 9.2 %slice.265 = bf16[1,128,1,1024]{3,1,2,0:T(8,128)(2,1)S(1)} slice(bf16[1,128,1,2048]{3,1,2,0:T(8,128)(2,1)S(1)} %get-tuple-element.19), slice={[0:1:1], [0:128:1], [0:1:1], [0:2048:2]} | slice | bytes 524288 | tf_op jit(solution)/shard_map/slice | solution.py:76
  212.2 1.1 pad_bitcast_fusion
  213.6 6.2 %gather_fusion.2 = bf16[2048,128]{1,0:T(8,128)(2,1)S(1)} fusion(bf16[128,2049]{0,1:T(8,128)(2,1)S(1)} %copy.23, s32[2048]{0:T(1024)S(1)} %fusion.96), kind=kCustom, calls=%fused_computation.2.clone | custom fusion | bytes 1056768 | tf_op jit(solution)/shard_map/jit(_take)/gather | solution.py:39
  220.3 0.8 slice.244
  221.2 0.8 slice.248
  222.2 0.8 slice.242
  224.7 0.8 fusion.75
  (57 shorter events, 6.6 us)
Async XLA Ops:
  9.2 12.6 %copy-start.3 = (s32[1,2048]{1,0:T(1,128)S(1)}, s32[1,2048]{1,0:T(1,128)}, u32[]{:S(2)}) copy-start(s32[1,2048]{1,0:T(1,128)} %param.10) | copy-start | bytes 24580
  9.2 31.5 %all-to-all-start = ((bf16[8,1,16,2,2048]{4,2,3,1,0:T(8,128)(2,1)}), bf16[8,1,16,2,2048]{4,2,3,1,0:T(8,128)(2,1)S(1)}, u32[]{:S(2)}, u32[]{:S(2)}) async-start(bf16[8,1,16,2,2048]{4,2,3,1,0:T(8,128)(2,1)} %stack.2), calls=%async_computation | async-start | bytes 2097152 | tf_op jit(solution)/shard_map/all_to_all | solution.py:10
  21.8 125.7 %all-gather.2.cloned.1.call-start = ((), (), s32[]{:S(2)}) async-start(), calls=%async_computation.1 | async-start | bytes 1179648 | tf_op jit(solution)/shard_map/all_gather | solution.py:68
  40.9 7.0 %copy-start.4 = (s32[1,2048]{1,0:T(1,128)S(1)}, s32[1,2048]{1,0:T(1,128)}, u32[]{:S(2)}) copy-start(s32[1,2048]{1,0:T(1,128)} %param.11) | copy-start | bytes 24580
  41.8 12.2 %collective-permute-start = (bf16[1,128,1,2048]{3,1,2,0:T(8,128)(2,1)S(1)}, bf16[1,128,1,2048]{3,1,2,0:T(8,128)(2,1)S(1)}, u32[]{:S(2)}, u32[]{:S(2)}) collective-permute-start(bf16[1,128,1,2048]{3,1,2,0:T(8,128)(2,1)S(1)} %get-tuple-element.27), channel_id=1, source_target_pairs={{0,8},{8,16},{16,24},{24,32},{32,40},{40,48},{48,56},{56,64},{64,7... | collective-permute-start | bytes 1572872 | tf_op jit(solution)/shard_map/ppermute | solution.py:22
  47.9 12.8 %collective-permute-start.1 = (bf16[1,128,1,2048]{3,1,2,0:T(8,128)(2,1)}, bf16[1,128,1,2048]{3,1,2,0:T(8,128)(2,1)S(1)}, u32[]{:S(2)}, u32[]{:S(2)}) collective-permute-start(bf16[1,128,1,2048]{3,1,2,0:T(8,128)(2,1)} %get-tuple-element.26), channel_id=1, source_target_pairs={{8,0},{16,8},{24,16},{32,24},{40,32},{48,40},{56,48},{64,56},{72,6... | collective-permute-start | bytes 1572872 | tf_op jit(solution)/shard_map/ppermute | solution.py:24
  67.6 1.4 copy-start.5
  71.6 0.7 copy-start.6
  147.5 8.6 %copy-start = (bf16[1,128,2,2048]{3,1,2,0:T(8,128)(2,1)S(1)}, bf16[1,128,2,2048]{3,1,2,0:T(8,128)(2,1)}, u32[]{:S(2)}) copy-start(bf16[1,128,2,2048]{3,1,2,0:T(8,128)(2,1)} %all-gather.2.cloned.1.call-done) | copy-start | bytes 3145732
  149.7 62.5 %collective-permute-start.2 = (bf16[1,128,2048]{2,1,0:T(8,128)(2,1)}, bf16[1,128,2048]{2,1,0:T(8,128)(2,1)}, u32[]{:S(2)}, u32[]{:S(2)}) collective-permute-start(bf16[1,128,2048]{2,1,0:T(8,128)(2,1)} %get-tuple-element.20), channel_id=1, source_target_pairs={{0,8},{8,16},{16,24},{24,32},{32,40},{40,48},{48,56},{56,64},{64,7... | collective-permute-start | bytes 1572872 | tf_op jit(solution)/shard_map/ppermute | solution.py:34
  221.2 1.8 copy-start.2
  223.7 1.0 copy-start.1
  223.8 0.9 copy-start.7
Sparse Core Ops, SparseCore 0:
  73.4 74.0 all-gather.1
